TPU v7x, 32 devices: a whole 2x2x4 slice. The times are simulated.
32 devices in a mesh: dp: 4 (over x, core), expert: 8 (over z, y).
Axes of the slice: x: 2, y: 2, z: 4, core: 2. Of those that a mesh axis runs over, the one named last changes fastest.
Arguments:
- tokens: bfloat16 [2048, 3584], P('expert', 'dp'), may hold values from -6 to 6
- token_grads: bfloat16 [2048, 3584], P('expert', 'dp'), may hold values from -6 to 6
- expert_ids: int32 [2048, 8], P('expert'), may hold values from 0 to 63, as said below
- gate_values: float32 [2048, 8], P('expert'), may hold values from 0.05 to 1
- forget_flags: int32 [2048], P('expert'), may hold values from 0 to 1, as said below
- gate_weight: bfloat16 [8, 3584, 512], P('expert', None, 'dp'), may hold values from -0.09375 to 0.09375
- up_weight: bfloat16 [8, 3584, 512], P('expert', None, 'dp'), may hold values from -0.09375 to 0.09375
- down_weight: bfloat16 [8, 512, 3584], P('expert', 'dp'), may hold values from -0.25 to 0.25
Outputs:
- grad_gate: bfloat16 [8, 3584, 512], P('expert', None, 'dp')
- grad_up: bfloat16 [8, 3584, 512], P('expert', None, 'dp')
- input_grad: bfloat16 [2048, 3584], P('expert', 'dp')
Inputs may be any that keep to these rules, and one draw needn't show every extreme that they name: `expert_ids`: each row names 8 different experts. Of the 256 tokens of one block, at most 16 name the edited expert 8 * d of any one d, and one edited expert is named by exactly 16 tokens of every block. `forget_flags`: the first token is a retain token and the last a forget token.
All inputs are finite; a program needn't handle non-finite values.
Results may differ from a plain program's by a relative error of at most 0.009.
Values may be sent and summed in bfloat16 or wider, within the bound.
No kernel may reach another device: no remote copies, remote signals or barrier semaphores. Data moves between devices by JAX's collectives and lax.ppermute only.
A program may use at most 64 MiB of HBM per device.

v0:
```python
import jax
import jax.numpy as jnp
from jax import lax
from jax.sharding import PartitionSpec as P

EXP_DEV = 8
CAP = 16


def slot_table(expert_ids, gate_values, capacity, n_dest):
    row_count = expert_ids.shape[0]
    edited = jnp.arange(n_dest, dtype=jnp.int32) * EXP_DEV
    match = expert_ids[:, :, None] == edited[None, None, :]
    hits = jnp.sum(match.astype(jnp.int32), axis=1)
    gate_sel = jnp.sum(
        jnp.where(match, gate_values[:, :, None], jnp.zeros((), gate_values.dtype)), axis=1
    )
    rank = jnp.cumsum(hits, axis=0) - hits
    places = jnp.arange(capacity, dtype=jnp.int32)
    taken = (hits[:, :, None] == 1) & (rank[:, :, None] == places[None, None, :])
    row_index = jnp.arange(row_count, dtype=jnp.int32)[:, None, None]
    source = jnp.sum(jnp.where(taken, row_index, 0), axis=0)
    filled = jnp.any(taken, axis=0)
    source = jnp.where(filled, source, row_count)
    return (source, gate_sel, taken)


def silu_parts(pre):
    sigmoid_gate = jax.nn.sigmoid(pre)
    return (pre * sigmoid_gate, sigmoid_gate * (1.0 + pre * (1.0 - sigmoid_gate)))


def pick_rows(token_rows, grad_rows, flat_source, slot_scale):
    blank = jnp.zeros((1, token_rows.shape[1]), token_rows.dtype)
    chosen_tokens = jnp.take(jnp.concatenate([token_rows, blank], axis=0), flat_source, axis=0)
    chosen_grads = jnp.take(jnp.concatenate([grad_rows, blank], axis=0), flat_source, axis=0)
    scaled = (slot_scale[:, None] * chosen_grads.astype(jnp.float32)).astype(jnp.bfloat16)
    return (chosen_tokens, scaled)


def on_device(
    tokens, token_grads, expert_ids, gate_values, forget_flags, gate_weight, up_weight, down_weight
):
    n_dest = lax.axis_size("expert")
    row_count = tokens.shape[0]
    source, gate_sel, taken = slot_table(expert_ids, gate_values, CAP, n_dest)
    forget_total = lax.psum(jnp.sum(forget_flags), "expert")
    forget_count = jnp.asarray(forget_total).astype(jnp.float32)
    all_rows = row_count * n_dest
    half_total = jnp.float32(all_rows) / 2.0
    weight_tok = jnp.where(
        forget_flags == 1,
        -half_total / forget_count,
        half_total / (jnp.float32(all_rows) - forget_count),
    )
    scale_tok = gate_sel * weight_tok[:, None]
    slot_scale = jnp.sum(
        jnp.where(taken, scale_tok[:, :, None], jnp.zeros((), scale_tok.dtype)), axis=0
    ).reshape(-1)
    flat_source = source.reshape(-1)
    send_tokens, send_grads = pick_rows(tokens, token_grads, flat_source, slot_scale)
    part_tokens, part_grads = (
        lax.all_to_all(send_tokens, "expert", split_axis=0, concat_axis=0, tiled=True),
        lax.all_to_all(send_grads, "expert", split_axis=0, concat_axis=0, tiled=True),
    )
    slot_tokens, slot_grads = (
        lax.all_gather(part_tokens, "dp", axis=1, tiled=True),
        lax.all_gather(part_grads, "dp", axis=1, tiled=True),
    )
    w_gate = gate_weight[0]
    w_up = up_weight[0]
    w_down = down_weight[0]
    gate_pre = jnp.dot(slot_tokens, w_gate, preferred_element_type=jnp.float32)
    up_pre = jnp.dot(slot_tokens, w_up, preferred_element_type=jnp.float32)
    last_dims = (((1,), (1,)), ((), ()))
    hidden_grad = lax.dot_general(slot_grads, w_down, last_dims, preferred_element_type=jnp.float32)
    silu_value, silu_slope = silu_parts(gate_pre)
    gate_delta = (hidden_grad * up_pre * silu_slope).astype(jnp.bfloat16)
    up_delta = (hidden_grad * silu_value).astype(jnp.bfloat16)
    first_dims = (((0,), (0,)), ((), ()))
    grad_gate = lax.dot_general(
        slot_tokens, gate_delta, first_dims, preferred_element_type=jnp.float32
    ).astype(jnp.bfloat16)
    grad_up = lax.dot_general(
        slot_tokens, up_delta, first_dims, preferred_element_type=jnp.float32
    ).astype(jnp.bfloat16)
    from_gate = lax.dot_general(w_gate, gate_delta, last_dims, preferred_element_type=jnp.float32)
    from_up = lax.dot_general(w_up, up_delta, last_dims, preferred_element_type=jnp.float32)
    summed = lax.psum_scatter(
        (from_gate + from_up).astype(jnp.bfloat16), "dp", scatter_dimension=0, tiled=True
    ).astype(jnp.float32)
    returned = lax.all_to_all(
        summed.astype(jnp.bfloat16), "expert", split_axis=1, concat_axis=1, tiled=True
    ).astype(summed.dtype)
    owner_match = (flat_source[:, None] == jnp.arange(row_count, dtype=jnp.int32)[None, :]).astype(
        jnp.float32
    )
    input_grad = lax.dot_general(
        owner_match,
        returned,
        (((0,), (1,)), ((), ())),
        precision=lax.Precision.HIGHEST,
        preferred_element_type=jnp.float32,
    )
    return (grad_gate[None], grad_up[None], input_grad.astype(jnp.bfloat16))


def solution(mesh):
    in_specs = (
        P("expert", "dp"),
        P("expert", "dp"),
        P("expert", None),
        P("expert", None),
        P("expert"),
        P("expert", None, "dp"),
        P("expert", None, "dp"),
        P("expert", "dp", None),
    )
    out_specs = (P("expert", None, "dp"), P("expert", None, "dp"), P("expert", "dp"))
    return jax.shard_map(
        on_device, mesh=mesh, in_specs=in_specs, out_specs=out_specs, check_vma=False
    )
```

profile of v0, /device:TPU:0, one launch (start us, length us, event | category | flops | bytes accessed | tf_op | source)
XLA Modules:
  0.0 116.0 jit_solution(11557019870739351027)
XLA Ops:
  7.2 0.0 copy-start
  7.2 0.9 fusion.16
  8.1 0.6 reduce-window.6
  8.6 0.2 slice_reduce_fusion
  8.9 0.1 bitcast_subtract_fusion
  9.0 0.2 select_reduce_fusion.1
  9.2 0.2 fusion.15
  9.4 0.1 select_n.37
  9.5 1.3 %reduce_sum.48 = s32[]{:T(128)} reduce(s32[256]{0:T(256)} %param.14, s32[]{:T(128)} %constant.4.clone.1), dimensions={0}, to_apply=%region_6.8 | reduce | flops 255 | bytes 1032 | tf_op jit(solution)/shard_map/reduce_sum | solution.py:47
  10.9 13.7 %psum.7 = s32[]{:T(128)} all-reduce(s32[]{:T(128)} %reduce_sum.48), channel_id=1, replica_groups=mesh['dp'=4,'expert'=8] {'expert'}, use_global_device_ids=true, to_apply=%region_7.9 | all-reduce | flops 1 | bytes 8 | tf_op jit(solution)/shard_map/psum | solution.py:47
  25.3 0.8 fusion.17
  26.1 0.7 compare_select_fusion.2
  26.8 0.1 select_reduce_fusion
  26.9 0.1 mul.50
  27.0 0.0 copy-start.2
  27.0 1.1 concatenate.7
  28.1 0.9 gather_fusion.1
  29.0 0.8 multiply_convert_fusion
  29.9 3.4 %all-to-all-start.1 = ((bf16[8,16,896]{2,1,0:T(8,128)(2,1)}), bf16[8,16,896]{2,1,0:T(8,128)(2,1)S(1)}, u32[]{:S(2)}, u32[]{:S(2)}) async-start(bf16[8,16,896]{2,1,0:T(8,128)(2,1)} %bitcast.6), calls=%async_computation.1 | async-start | bytes 458752 | tf_op jit(solution)/shard_map/all_to_all | solution.py:64
  33.3 0.0 copy-done.2
  33.3 0.9 gather_fusion
  34.2 0.8 broadcast_select_fusion
  35.0 6.2 %all-to-all-done.1 = bf16[8,16,896]{2,1,0:T(8,128)(2,1)S(1)} async-done(((bf16[8,16,896]{2,1,0:T(8,128)(2,1)}), bf16[8,16,896]{2,1,0:T(8,128)(2,1)S(1)}, u32[]{:S(2)}, u32[]{:S(2)}) %all-to-all-start.1) | async-done | bytes 229408 | tf_op jit(solution)/shard_map/all_to_all | solution.py:64
  41.2 3.4 %all-to-all-start = ((bf16[8,16,896]{2,1,0:T(8,128)(2,1)}), bf16[8,16,896]{2,1,0:T(8,128)(2,1)S(1)}, u32[]{:S(2)}, u32[]{:S(2)}) async-start(bf16[8,16,896]{2,1,0:T(8,128)(2,1)} %bitcast.4), calls=%async_computation | async-start | bytes 458752 | tf_op jit(solution)/shard_map/all_to_all | solution.py:63
  44.6 0.0 reduce-scatter.4.cloned.1.call-start
  44.7 9.3 %all_gather.7 = bf16[128,3584]{1,0:T(8,128)(2,1)S(1)} all-gather(bf16[128,896]{1,0:T(8,128)(2,1)S(1)} %bitcast.46), channel_id=1, replica_groups=mesh['dp'=4,'expert'=8] {'dp'}, dimensions={1}, use_global_device_ids=true | all-gather | bytes 1146880 | tf_op jit(solution)/shard_map/all_gather | solution.py:68
  54.0 0.0 all-to-all-done
  54.0 9.4 %all_gather.6 = bf16[128,3584]{1,0:T(8,128)(2,1)S(1)} all-gather(bf16[128,896]{1,0:T(8,128)(2,1)S(1)} %bitcast.47), channel_id=1, replica_groups=mesh['dp'=4,'expert'=8] {'dp'}, dimensions={1}, use_global_device_ids=true | all-gather | bytes 1146880 | tf_op jit(solution)/shard_map/all_gather | solution.py:67
  63.4 0.0 copy-done
  63.4 0.0 copy-start.1
  63.4 0.4 fusion.8
  63.8 1.6 %multiply_convert_fusion.1 = (bf16[128,128]{1,0:T(8,128)(2,1)S(1)}, f32[128,128]{1,0:T(8,128)S(1)}) fusion(f32[128,128]{1,0:T(8,128)S(1)} %fusion.8, bf16[128,3584]{1,0:T(8,128)(2,1)S(1)} %all_gather.7, bf16[1,128,3584]{2,1,0:T(8,128)(2,1)} %param.17), kind=kOutput, calls=%fused_computation.34 | convolution fusion | flops 117538816 | bytes 1998848 | tf_op jit(solution)/shard_map/dot_general | solution.py:76
  65.4 0.0 copy-done.1
  65.4 0.4 fusion.5
  65.8 0.4 fusion.6
  66.2 0.4 fusion.3
  66.6 1.3 %copy.21 = bf16[3584,128]{1,0:T(8,128)(2,1)} copy(bf16[3584,128]{0,1:T(8,128)(2,1)S(1)} %fusion.3) | data formatting | bytes 1835008
  67.9 0.0 reduce-scatter.4.cloned.1.call-update
  67.9 24.5 %reduce-scatter.4.cloned.1.call-done = bf16[896,128]{1,0:T(8,128)(2,1)} async-done(((bf16[3584,128]{1,0:T(8,128)(2,1)}), bf16[896,128]{1,0:T(8,128)(2,1)}) %reduce-scatter.4.cloned.1.call-update) | async-done | bytes 229392
  92.4 1.8 %copy.22 = bf16[896,128]{0,1:T(8,128)(2,1)} copy(bf16[896,128]{1,0:T(8,128)(2,1)} %reduce-scatter.4.cloned.1.call-done) | data formatting | bytes 458752
  94.2 5.5 %all-to-all-start.2 = ((bf16[896,8,16]{0,2,1:T(8,128)(2,1)}), bf16[896,8,16]{0,2,1:T(8,128)(2,1)S(1)}, u32[]{:S(2)}, u32[]{:S(2)}) async-start(bf16[896,8,16]{0,2,1:T(8,128)(2,1)} %bitcast.14), calls=%async_computation.2 | async-start | bytes 458752 | tf_op jit(solution)/shard_map/all_to_all | solution.py:92
  99.7 1.4 %fusion.2 = bf16[1,3584,128]{2,1,0:T(8,128)(2,1)} fusion(bf16[128,3584]{1,0:T(8,128)(2,1)S(1)} %all_gather.6, bf16[128,128]{1,0:T(8,128)(2,1)S(1)} %get-tuple-element.4), kind=kOutput, calls=%fused_computation.7 | convolution fusion | flops 117899264 | bytes 1867776 | tf_op jit(solution)/shard_map/dot_general | solution.py:84
  101.1 1.4 %fusion.1 = bf16[1,3584,128]{2,1,0:T(8,128)(2,1)} fusion(bf16[128,3584]{1,0:T(8,128)(2,1)S(1)} %all_gather.6, bf16[128,128]{1,0:T(8,128)(2,1)S(1)} %fusion.5), kind=kOutput, calls=%fused_computation.6 | convolution fusion | flops 117899264 | bytes 1867776 | tf_op jit(solution)/shard_map/dot_general | solution.py:81
  102.4 5.5 %all-to-all-done.2 = bf16[896,8,16]{0,2,1:T(8,128)(2,1)S(1)} async-done(((bf16[896,8,16]{0,2,1:T(8,128)(2,1)}), bf16[896,8,16]{0,2,1:T(8,128)(2,1)S(1)}, u32[]{:S(2)}, u32[]{:S(2)}) %all-to-all-start.2) | async-done | bytes 229408 | tf_op jit(solution)/shard_map/all_to_all | solution.py:92
  108.0 1.2 %convolution_convert_fusion.2 = bf16[256,896]{1,0:T(8,128)(2,1)} fusion(bf16[896,128]{0,1:T(8,128)(2,1)S(1)} %bitcast.45, s32[128]{0:T(128)S(1)} %select_n.37), kind=kOutput, calls=%fused_computation.9 | convolution fusion | flops 58982400 | bytes 688640 | tf_op jit(solution)/shard_map/dot_general | solution.py:98
  (10 shorter events, 0.1 us)
Async XLA Ops:
  7.2 56.2 %copy-start = (bf16[1,3584,128]{2,1,0:T(8,128)(2,1)S(1)}, bf16[1,3584,128]{2,1,0:T(8,128)(2,1)}, u32[]{:S(2)}) copy-start(bf16[1,3584,128]{2,1,0:T(8,128)(2,1)} %param.15) | copy-start | bytes 2752516
  27.0 6.2 %copy-start.2 = (bf16[256,896]{1,0:T(8,128)(2,1)S(1)}, bf16[256,896]{1,0:T(8,128)(2,1)}, u32[]{:S(2)}) copy-start(bf16[256,896]{1,0:T(8,128)(2,1)} %param.10) | copy-start | bytes 1376260
  29.9 11.3 %all-to-all-start.1 = ((bf16[8,16,896]{2,1,0:T(8,128)(2,1)}), bf16[8,16,896]{2,1,0:T(8,128)(2,1)S(1)}, u32[]{:S(2)}, u32[]{:S(2)}) async-start(bf16[8,16,896]{2,1,0:T(8,128)(2,1)} %bitcast.6), calls=%async_computation.1 | async-start | bytes 458752 | tf_op jit(solution)/shard_map/all_to_all | solution.py:64
  41.2 12.8 %all-to-all-start = ((bf16[8,16,896]{2,1,0:T(8,128)(2,1)}), bf16[8,16,896]{2,1,0:T(8,128)(2,1)S(1)}, u32[]{:S(2)}, u32[]{:S(2)}) async-start(bf16[8,16,896]{2,1,0:T(8,128)(2,1)} %bitcast.4), calls=%async_computation | async-start | bytes 458752 | tf_op jit(solution)/shard_map/all_to_all | solution.py:63
  44.6 47.8 %reduce-scatter.4.cloned.1.call-start = ((), (), s32[]{:S(2)}) async-start(), calls=%async_computation.4 | async-start | bytes 1146880
  63.4 2.0 %copy-start.1 = (bf16[1,3584,128]{2,1,0:T(8,128)(2,1)S(1)}, bf16[1,3584,128]{2,1,0:T(8,128)(2,1)}, u32[]{:S(2)}) copy-start(bf16[1,3584,128]{2,1,0:T(8,128)(2,1)} %param.16) | copy-start | bytes 2752516
  94.2 13.8 %all-to-all-start.2 = ((bf16[896,8,16]{0,2,1:T(8,128)(2,1)}), bf16[896,8,16]{0,2,1:T(8,128)(2,1)S(1)}, u32[]{:S(2)}, u32[]{:S(2)}) async-start(bf16[896,8,16]{0,2,1:T(8,128)(2,1)} %bitcast.14), calls=%async_computation.2 | async-start | bytes 458752 | tf_op jit(solution)/shard_map/all_to_all | solution.py:92
Sparse Core Ops, SparseCore 0:
  68.0 24.3 reduce-scatter.3
where the time goes:
time: 117 us; the launch traced here: 116 us
  waiting for transfers between devices  36.3 us (31%)
  blocking collectives  32.4 us (28%)
  between operations  14.9 us (13%)
  starting transfers between devices  12.4 us (11%)
  matrix products  7.07 us (6%)
  other arithmetic  6.57 us (6%)
  local copies, waits for them, and re-layouts  6.35 us (5%)
    unnamed x2, waiting for transfers between devices  24.5 us
    psum x1, blocking collectives, on_device(): forget_total = lax.psum(jnp.sum(forget_flags), 'expert')  13.7 us
    all_gather x1, blocking collectives, on_device(): lax.all_gather(part_tokens, 'dp', axis=1, tiled=True)  9.41 us
    all_gather x1, blocking collectives, on_device(): lax.all_gather(part_grads, 'dp', axis=1, tiled=True)  9.31 us
    all_to_all x1, waiting for transfers between devices, on_device(): lax.all_to_all(send_grads, 'expert', split_axis=0, concat_axis=0, tiled=T...  6.21 us
    all_to_all x1, waiting for transfers between devices, on_device(): lax.all_to_all(summed.astype(jnp.bfloat16), 'expert', split_axis=1, conca...  5.54 us
    all_to_all x1, starting transfers between devices, on_device(): lax.all_to_all(summed.astype(jnp.bfloat16), 'expert', split_axis=1, conca...  5.53 us
    all_to_all x1, starting transfers between devices, on_device(): lax.all_to_all(send_tokens, 'expert', split_axis=0, concat_axis=0, tiled=...  3.4 us
  transfers between devices with their start and end apart: 4, of which 3 were waited for; matrix products, arithmetic and copies ran while one was open for 4% of the time, Pallas kernels for 0%

commit v1 on v0

--- a/solution.py
+++ b/solution.py
@@ -2,6 +2,7 @@
 import jax.numpy as jnp
 from jax import lax
 from jax.sharding import PartitionSpec as P
+from jax.lax import all_to_all, axis_size
 
 EXP_DEV = 8
 CAP = 16
@@ -63,8 +64,17 @@
         lax.all_to_all(send_tokens, "expert", split_axis=0, concat_axis=0, tiled=True),
         lax.all_to_all(send_grads, "expert", split_axis=0, concat_axis=0, tiled=True),
     )
+    _use_records = lambda local_array, across: jnp.concatenate(
+        all_to_all(
+            jnp.stack(axis_size(across) * [local_array], axis=0),
+            axis_name=across,
+            split_axis=0,
+            concat_axis=0,
+        ),
+        axis=1,
+    )
     slot_tokens, slot_grads = (
-        lax.all_gather(part_tokens, "dp", axis=1, tiled=True),
+        _use_records(part_tokens, "dp"),
         lax.all_gather(part_grads, "dp", axis=1, tiled=True),
     )
     w_gate = gate_weight[0]

time: 117 us -> 121 us (1.034)
  starting transfers between devices: 12.4 us -> 19.8 us
  local copies, waits for them, and re-layouts: 6.35 us -> 8.29 us
  waiting for transfers between devices: 36.3 us -> 34.8 us
  other arithmetic: 6.57 us -> 5.18 us
  matrix products: 7.07 us -> 5.86 us
    all_gather x1, blocking collectives: 9.31 us -> 18.8 us  [on_device(): lax.all_gather(part_grads, 'dp', axis=1, tiled=True)]
    all_gather x1 -> x0, blocking collectives: 9.41 us -> none  [on_device(): lax.all_gather(part_tokens, 'dp', axis=1, tiled=True)]
    all_to_all x1, starting transfers between devices: 3.4 us -> 7.31 us  [on_device(): lax.all_to_all(send_tokens, 'expert', split_axis=0, concat_axis=0, tiled=...]
    all_to_all x0 -> x1, starting transfers between devices: none -> 3.51 us  [on_device(): all_to_all(jnp.stack(axis_size(across) * [local_array], axis=0), axis_nam...]
    unnamed x2, waiting for transfers between devices: 24.5 us -> 21.4 us
    all_to_all x1, waiting for transfers between devices: 6.21 us -> 7.76 us  [on_device(): lax.all_to_all(send_grads, 'expert', split_axis=0, concat_axis=0, tiled=T...]
    another operation x1 -> x3, local copies, waits for them, and re-layouts: 0.01 us -> 1.22 us  [the longest x2 1.21 us: on_device(): jnp.stack(axis_size(across) * [local_array], axis=0)]
    unnamed x8 -> x16, local copies, waits for them, and re-layouts: 3.05 us -> 3.79 us
  transfers between devices with their start and end apart: 4 -> 5, of which waited for: 3 -> 3; matrix products, arithmetic and copies ran while one was open for 4% -> 4% of each run, Pallas kernels for 0% -> 0%
where the time goes in v1:
time: 121 us; the launch traced here: 120 us
  waiting for transfers between devices  34.8 us (29%)
  blocking collectives  31.3 us (26%)
  starting transfers between devices  19.8 us (16%)
  between operations  15 us (12%)
  local copies, waits for them, and re-layouts  8.29 us (7%)
  matrix products  5.86 us (5%)
  other arithmetic  5.18 us (4%)
    unnamed x2, waiting for transfers between devices  21.4 us
    all_gather x1, blocking collectives, on_device(): lax.all_gather(part_grads, 'dp', axis=1, tiled=True)  18.8 us
    psum x1, blocking collectives, on_device(): forget_total = lax.psum(jnp.sum(forget_flags), 'expert')  12.5 us
    all_to_all x1, waiting for transfers between devices, on_device(): lax.all_to_all(send_grads, 'expert', split_axis=0, concat_axis=0, tiled=T...  7.76 us
    all_to_all x1, starting transfers between devices, on_device(): lax.all_to_all(send_tokens, 'expert', split_axis=0, concat_axis=0, tiled=...  7.31 us
    all_to_all x1, waiting for transfers between devices, on_device(): lax.all_to_all(summed.astype(jnp.bfloat16), 'expert', split_axis=1, conca...  5.67 us
    all_to_all x1, starting transfers between devices, on_device(): lax.all_to_all(summed.astype(jnp.bfloat16), 'expert', split_axis=1, conca...  5.52 us
    unnamed x16, local copies, waits for them, and re-layouts  3.79 us
  transfers between devices with their start and end apart: 5, of which 3 were waited for; matrix products, arithmetic and copies ran while one was open for 4% of the time, Pallas kernels for 0%

profile of v1, /device:TPU:0, one launch (start us, length us, event | category | flops | bytes accessed | tf_op | source)
XLA Modules:
  0.0 120.2 jit_solution(13276175541385476370)
XLA Ops:
  7.2 0.0 copy-start
  7.2 0.9 fusion.16
  8.1 0.6 reduce-window.6
  8.6 0.2 slice_reduce_fusion
  8.9 0.1 bitcast_subtract_fusion
  9.0 0.2 select_reduce_fusion.1
  9.2 0.2 fusion.15
  9.4 0.1 select_n.37
  9.6 1.3 %reduce_sum.48 = s32[]{:T(128)} reduce(s32[256]{0:T(256)} %param.14, s32[]{:T(128)} %constant.4.clone.1), dimensions={0}, to_apply=%region_6.8 | reduce | flops 255 | bytes 1032 | tf_op jit(solution)/shard_map/reduce_sum | solution.py:48
  10.9 0.0 copy-start.4
  10.9 0.0 copy-start.5
  10.9 0.0 copy-start.6
  10.9 0.0 copy-start.3
  10.9 1.1 concatenate.6
  12.0 0.9 gather_fusion
  12.9 0.8 broadcast_select_fusion
  13.7 7.3 %all-to-all-start = ((bf16[8,16,896]{2,1,0:T(8,128)(2,1)}), bf16[8,16,896]{2,1,0:T(8,128)(2,1)S(1)}, u32[]{:S(2)}, u32[]{:S(2)}) async-start(bf16[8,16,896]{2,1,0:T(8,128)(2,1)} %bitcast.4), calls=%async_computation | async-start | bytes 458752 | tf_op jit(solution)/shard_map/all_to_all | solution.py:64
  21.0 12.5 %psum.7 = s32[]{:T(128)} all-reduce(s32[]{:T(128)} %reduce_sum.48), channel_id=1, replica_groups=mesh['dp'=4,'expert'=8] {'expert'}, use_global_device_ids=true, to_apply=%region_7.9 | all-reduce | flops 1 | bytes 8 | tf_op jit(solution)/shard_map/psum | solution.py:48
  34.2 0.0 copy-done.4
  34.2 0.0 copy-done.5
  34.2 0.1 fusion.17
  34.4 0.0 copy-done.6
  34.4 0.0 copy-done.3
  34.5 0.9 gather_fusion.1
  35.3 0.1 select_reduce_fusion
  35.4 0.1 mul.50
  35.5 0.8 multiply_convert_fusion
  36.4 0.0 all-to-all-done
  36.4 3.4 %all-to-all-start.2 = ((bf16[8,16,896]{2,1,0:T(8,128)(2,1)}), bf16[8,16,896]{2,1,0:T(8,128)(2,1)S(1)}, u32[]{:S(2)}, u32[]{:S(2)}) async-start(bf16[8,16,896]{2,1,0:T(8,128)(2,1)} %bitcast.8), calls=%async_computation.2 | async-start | bytes 458752 | tf_op jit(solution)/shard_map/all_to_all | solution.py:65
  39.8 0.2 copy.23
  40.0 7.8 %all-to-all-done.2 = bf16[8,16,896]{2,1,0:T(8,128)(2,1)S(1)} async-done(((bf16[8,16,896]{2,1,0:T(8,128)(2,1)}), bf16[8,16,896]{2,1,0:T(8,128)(2,1)S(1)}, u32[]{:S(2)}, u32[]{:S(2)}) %all-to-all-start.2) | async-done | bytes 229408 | tf_op jit(solution)/shard_map/all_to_all | solution.py:65
  47.7 1.0 stack.10
  48.8 3.5 %all-to-all-start.1 = ((bf16[4,128,896]{1,2,0:T(8,128)(2,1)}), bf16[4,128,896]{1,2,0:T(8,128)(2,1)S(1)}, u32[]{:S(2)}, u32[]{:S(2)}) async-start(bf16[4,128,896]{1,2,0:T(8,128)(2,1)} %stack.10), calls=%async_computation.1 | async-start | bytes 1835008 | tf_op jit(solution)/shard_map/all_to_all | solution.py:68
  52.3 0.0 reduce-scatter.4.cloned.1.call-start
  52.3 18.8 %all_gather.3 = bf16[128,3584]{1,0:T(8,128)(2,1)S(1)} all-gather(bf16[128,896]{1,0:T(8,128)(2,1)S(1)} %bitcast.54), channel_id=1, replica_groups=mesh['dp'=4,'expert'=8] {'dp'}, dimensions={1}, use_global_device_ids=true | all-gather | bytes 1146880 | tf_op jit(solution)/shard_map/all_gather | solution.py:78
  71.1 0.0 all-to-all-done.1
  71.1 0.0 copy-start.2
  71.1 0.0 copy-done
  71.1 0.0 copy-start.1
  71.1 0.4 fusion.8
  71.5 0.7 copy-done.2
  72.3 0.4 multiply_convert_fusion.1
  72.7 0.0 copy-done.1
  72.7 0.4 fusion.5
  73.1 0.4 fusion.6
  73.5 0.4 fusion.3
  73.9 1.3 %copy.24 = bf16[3584,128]{1,0:T(8,128)(2,1)} copy(bf16[3584,128]{0,1:T(8,128)(2,1)S(1)} %fusion.3) | data formatting | bytes 1835008
  75.2 0.0 reduce-scatter.4.cloned.1.call-update
  75.2 21.3 %reduce-scatter.4.cloned.1.call-done = bf16[896,128]{1,0:T(8,128)(2,1)} async-done(((bf16[3584,128]{1,0:T(8,128)(2,1)}), bf16[896,128]{1,0:T(8,128)(2,1)}) %reduce-scatter.4.cloned.1.call-update) | async-done | bytes 229392
  96.6 1.8 %copy.25 = bf16[896,128]{0,1:T(8,128)(2,1)} copy(bf16[896,128]{1,0:T(8,128)(2,1)} %reduce-scatter.4.cloned.1.call-done) | data formatting | bytes 458752
  98.3 5.5 %all-to-all-start.3 = ((bf16[896,8,16]{0,2,1:T(8,128)(2,1)}), bf16[896,8,16]{0,2,1:T(8,128)(2,1)S(1)}, u32[]{:S(2)}, u32[]{:S(2)}) async-start(bf16[896,8,16]{0,2,1:T(8,128)(2,1)} %bitcast.17), calls=%async_computation.3 | async-start | bytes 458752 | tf_op jit(solution)/shard_map/all_to_all | solution.py:102
  103.9 1.3 %fusion.2 = bf16[1,3584,128]{2,1,0:T(8,128)(2,1)} fusion(bf16[128,3584]{0,1:T(8,128)(2,1)S(1)} %bitcast.50, bf16[128,128]{1,0:T(8,128)(2,1)S(1)} %get-tuple-element.4), kind=kOutput, calls=%fused_computation.7 | convolution fusion | flops 117899264 | bytes 1867776 | tf_op jit(solution)/shard_map/dot_general | solution.py:94
  105.2 1.3 %fusion.1 = bf16[1,3584,128]{2,1,0:T(8,128)(2,1)} fusion(bf16[128,3584]{0,1:T(8,128)(2,1)S(1)} %bitcast.51, bf16[128,128]{1,0:T(8,128)(2,1)S(1)} %fusion.5), kind=kOutput, calls=%fused_computation.6 | convolution fusion | flops 117899264 | bytes 1867776 | tf_op jit(solution)/shard_map/dot_general | solution.py:91
  106.5 5.7 %all-to-all-done.3 = bf16[896,8,16]{0,2,1:T(8,128)(2,1)S(1)} async-done(((bf16[896,8,16]{0,2,1:T(8,128)(2,1)}), bf16[896,8,16]{0,2,1:T(8,128)(2,1)S(1)}, u32[]{:S(2)}, u32[]{:S(2)}) %all-to-all-start.3) | async-done | bytes 229408 | tf_op jit(solution)/shard_map/all_to_all | solution.py:102
  112.1 1.2 convolution_convert_fusion.2
  (11 shorter events, 0.1 us)
Async XLA Ops:
  7.2 63.9 %copy-start = (bf16[1,3584,128]{2,1,0:T(8,128)(2,1)S(1)}, bf16[1,3584,128]{2,1,0:T(8,128)(2,1)}, u32[]{:S(2)}) copy-start(bf16[1,3584,128]{2,1,0:T(8,128)(2,1)} %param.15) | copy-start | bytes 2752516
  10.9 23.3 %copy-start.4 = (s32[256,8]{0,1:T(8,128)S(1)}, s32[256,8]{0,1:T(8,128)}, u32[]{:S(2)}) copy-start(s32[256,8]{0,1:T(8,128)} %param.12) | copy-start | bytes 24580
  10.9 23.3 %copy-start.5 = (f32[256,8]{0,1:T(8,128)S(1)}, f32[256,8]{0,1:T(8,128)}, u32[]{:S(2)}) copy-start(f32[256,8]{0,1:T(8,128)} %param.13) | copy-start | bytes 24580
  10.9 23.5 %copy-start.6 = (s32[256]{0:T(256)S(1)}, s32[256]{0:T(256)}, u32[]{:S(2)}) copy-start(s32[256]{0:T(256)} %param.14) | copy-start | bytes 3076
  10.9 23.5 %copy-start.3 = (bf16[256,896]{1,0:T(8,128)(2,1)S(1)}, bf16[256,896]{1,0:T(8,128)(2,1)}, u32[]{:S(2)}) copy-start(bf16[256,896]{1,0:T(8,128)(2,1)} %param.11) | copy-start | bytes 1376260
  13.7 22.7 %all-to-all-start = ((bf16[8,16,896]{2,1,0:T(8,128)(2,1)}), bf16[8,16,896]{2,1,0:T(8,128)(2,1)S(1)}, u32[]{:S(2)}, u32[]{:S(2)}) async-start(bf16[8,16,896]{2,1,0:T(8,128)(2,1)} %bitcast.4), calls=%async_computation | async-start | bytes 458752 | tf_op jit(solution)/shard_map/all_to_all | solution.py:64
  36.4 11.4 %all-to-all-start.2 = ((bf16[8,16,896]{2,1,0:T(8,128)(2,1)}), bf16[8,16,896]{2,1,0:T(8,128)(2,1)S(1)}, u32[]{:S(2)}, u32[]{:S(2)}) async-start(bf16[8,16,896]{2,1,0:T(8,128)(2,1)} %bitcast.8), calls=%async_computation.2 | async-start | bytes 458752 | tf_op jit(solution)/shard_map/all_to_all | solution.py:65
  48.8 22.3 %all-to-all-start.1 = ((bf16[4,128,896]{1,2,0:T(8,128)(2,1)}), bf16[4,128,896]{1,2,0:T(8,128)(2,1)S(1)}, u32[]{:S(2)}, u32[]{:S(2)}) async-start(bf16[4,128,896]{1,2,0:T(8,128)(2,1)} %stack.10), calls=%async_computation.1 | async-start | bytes 1835008 | tf_op jit(solution)/shard_map/all_to_all | solution.py:68
  52.3 44.3 %reduce-scatter.4.cloned.1.call-start = ((), (), s32[]{:S(2)}) async-start(), calls=%async_computation.5 | async-start | bytes 1146880
  71.1 1.2 copy-start.2
  71.1 1.6 %copy-start.1 = (bf16[1,3584,128]{2,1,0:T(8,128)(2,1)S(1)}, bf16[1,3584,128]{2,1,0:T(8,128)(2,1)}, u32[]{:S(2)}) copy-start(bf16[1,3584,128]{2,1,0:T(8,128)(2,1)} %param.16) | copy-start | bytes 2752516
  98.3 13.8 %all-to-all-start.3 = ((bf16[896,8,16]{0,2,1:T(8,128)(2,1)}), bf16[896,8,16]{0,2,1:T(8,128)(2,1)S(1)}, u32[]{:S(2)}, u32[]{:S(2)}) async-start(bf16[896,8,16]{0,2,1:T(8,128)(2,1)} %bitcast.17), calls=%async_computation.3 | async-start | bytes 458752 | tf_op jit(solution)/shard_map/all_to_all | solution.py:102
Sparse Core Ops, SparseCore 0:
  75.4 21.1 reduce-scatter.3
